TPU v7x, 512 devices: a whole 4x8x8 slice. The times are simulated.
512 devices in a mesh: space: 32 (over y_lo, z), field: 16 (over x, y_hi, core).
Axes of the slice: x: 4, y: 8 (y_hi: 2, y_lo: 4; y = y_hi * 4 + y_lo), z: 8, core: 2. Of those that a mesh axis runs over, the one named last changes fastest.
Arguments:
- fields: float32 [16, 1024, 6144], P('field', 'space'), may hold values from -6 to 6
- zone_ids: int32 [1024, 6144], P('space'), may hold values from 0 to 7
- diffusivity: float32 [16, 8], P('field'), may hold values from 0.3 to 3
- heat_rate: float32 [15], replicated, may hold values from 0.3 to 1.5
- weight_in: bfloat16 [384, 16], replicated, may hold values from -1.5 to 1.5
- bias_in: float32 [384], replicated, may hold values from -3 to 3
- weight_mid: bfloat16 [384, 384], replicated, may hold values from -0.3125 to 0.3125
- bias_mid: float32 [384], replicated, may hold values from -3 to 3
- weight_out: bfloat16 [16, 384], replicated, may hold values from -0.3125 to 0.3125
- bias_out: float32 [16], replicated, may hold values from -2 to 2
Outputs:
- new_fields: float32 [16, 1024, 6144], P('field', 'space')
All inputs are finite; a program needn't handle non-finite values.
Results may differ from a plain program's by a relative error of at most 0.005.
Values may be sent and summed in bfloat16 or wider, within the bound.
No kernel may reach another device: no remote copies, remote signals or barrier semaphores. Data moves between devices by JAX's collectives and lax.ppermute only.
A program may use at most 64 MiB of HBM per device.

v0:
```python
import jax
import jax.numpy as jnp
from jax import lax
from jax.sharding import PartitionSpec as P

FIELDS = 16
SWEEPS = 3
ROWS_BLK = 1024
RELAX_WEIGHTS = (0.8, 1.25, 0.95)


def extended(cells, sides, width):
    for axis, dim in sides:
        count = lax.axis_size(axis)
        ends = count - 1
        head = lax.slice_in_dim(cells, 0, width, axis=dim)
        tail = lax.slice_in_dim(cells, cells.shape[dim] - width, cells.shape[dim], axis=dim)
        cells = jnp.concatenate(
            [
                lax.ppermute(tail, axis, [(i, (i + 1) % count) for i in range(ends)]),
                cells,
                lax.ppermute(head, axis, [((i + 1) % count, i) for i in range(ends)]),
            ],
            axis=dim,
        )
    return cells


def from_root(block, axis, holder):
    block = jnp.where(lax.axis_index(axis) == holder, block, jnp.zeros_like(block))
    return lax.psum(block, axis)


def relax_step(padded, source, coef_pad, weight):
    middle = padded[:, 1:-1]
    coef_mid = coef_pad[:, 1:-1]
    face_north = 0.5 * (coef_mid + coef_pad[:, 2:])
    face_south = 0.5 * (coef_mid + coef_pad[:, :-2])
    face_east = 0.5 * (coef_mid + jnp.roll(coef_mid, -1, 2))
    face_west = 0.5 * (coef_mid + jnp.roll(coef_mid, 1, 2))
    diagonal = 1.0 + face_north + face_south + face_east + face_west
    image = diagonal * middle - face_north * padded[:, 2:] - face_south * padded[:, :-2]
    image = image - face_east * jnp.roll(middle, -1, 2) - face_west * jnp.roll(middle, 1, 2)
    return middle + weight * (source - image) / diagonal


def lookup(zone_ids, diffusivity):
    coefs = jnp.zeros((diffusivity.shape[0],) + zone_ids.shape, jnp.float32)
    for number in range(diffusivity.shape[1]):
        coefs = coefs + jnp.where(
            (zone_ids == number)[None], diffusivity[:, number][:, None, None], jnp.float32(0.0)
        )
    return coefs


def on_device(
    fields,
    zone_ids,
    diffusivity,
    heat_rate,
    weight_in,
    bias_in,
    weight_mid,
    bias_mid,
    weight_out,
    bias_out,
):
    count_here, rows_here, columns = fields.shape
    coefs = lookup(zone_ids, diffusivity)
    stacked = extended(jnp.stack([fields, coefs]), (("space", 2),), 1)
    coef_pad = stacked[1]
    state = relax_step(stacked[0], fields, coef_pad, RELAX_WEIGHTS[0])
    for number in range(1, SWEEPS):
        padded = extended(state, (("space", 1),), 1)
        state = relax_step(padded, fields, coef_pad, RELAX_WEIGHTS[number])
    span = ROWS_BLK * lax.axis_size("field")
    blocks = rows_here * columns // span
    by_block = state.reshape(count_here, blocks, span)

    def one_block(row_block):
        hidden = jax.nn.silu(
            jnp.dot(weight_in, row_block, preferred_element_type=jnp.float32) + bias_in[:, None]
        ).astype(jnp.bfloat16)
        hidden = jax.nn.silu(
            jnp.dot(weight_mid, hidden, preferred_element_type=jnp.float32) + bias_mid[:, None]
        ).astype(jnp.bfloat16)
        return (
            jnp.dot(weight_out, hidden, preferred_element_type=jnp.float32) + bias_out[:, None]
        ).astype(jnp.bfloat16)

    moved = jnp.moveaxis(
        lax.all_to_all(
            by_block.astype(jnp.bfloat16), "field", split_axis=2, concat_axis=0, tiled=True
        ),
        1,
        0,
    )
    change = jnp.moveaxis(lax.map(one_block, moved), 0, 1)
    change = lax.all_to_all(change, "field", split_axis=0, concat_axis=2, tiled=True).astype(
        jnp.float32
    )
    heat_local = by_block[-1] + change[-1]
    heat_new = from_root(heat_local, "field", lax.axis_size("field") - 1)
    first_field = lax.axis_index("field") * count_here
    rate_pad = jnp.concatenate([heat_rate, jnp.zeros((1,), jnp.float32)], 0)
    rate_here = lax.dynamic_slice_in_dim(rate_pad, first_field, count_here)
    factor = jnp.exp(rate_here[:, None, None] * jnp.tanh(heat_new)[None])
    result = by_block + (change * factor).astype(jnp.bfloat16).astype(jnp.float32)
    field_ids = first_field + jnp.arange(count_here, dtype=jnp.int32)
    result = jnp.where((field_ids == FIELDS - 1)[:, None, None], heat_new[None], result)
    return result.reshape(count_here, rows_here, columns)


def solution(mesh):
    return jax.shard_map(
        on_device,
        mesh=mesh,
        in_specs=(
            P("field", "space", None),
            P("space", None),
            P("field", None),
            P(),
            P(),
            P(),
            P(),
            P(),
            P(),
            P(),
        ),
        out_specs=P("field", "space", None),
        check_vma=False,
    )
```

profile of v0, /device:TPU:1, one launch (start us, length us, event | category | flops | bytes accessed | tf_op | source)
XLA Modules:
  0.0 460.7 jit_solution(11899596553922637642)
XLA Ops:
  6.5 1.6 fusion.65
  8.2 6.7 %add_bitcast_fusion = f32[1,1,32,6144]{3,2,1,0:T(8,128)S(1)} fusion(s32[32,6144]{1,0:T(8,128)} %param.13, f32[]{:T(128)} %bitcast.13, f32[]{:T(128)} %bitcast.12, f32[]{:T(128)} %bitcast.11, f32[]{:T(128)} %bitcast.10, f32[]{:T(128)} %bitcast.9, f32[]{:T(128)} %bitcast.8, f32[]{:T(128)} %bitcast.7, f32[]{:T(128)} %bitcast.6), kind=kLoop, calls=%fused_computation.80 | loop fusion | flops 4521984 | bytes 1572896 | tf_op jit(solution)/shard_map/stack | solution.py:70
  14.9 4.8 %collective-permute-start = (f32[2,1,1,6144]{3,2,1,0:T(1,128)S(1)}, f32[2,1,1,6144]{3,2,1,0:T(1,128)S(1)}, u32[]{:S(2)}, u32[]{:S(2)}) collective-permute-start(f32[2,1,1,6144]{3,2,1,0:T(1,128)S(1)} %get-tuple-element.78), channel_id=1, source_target_pairs={{0,16},{16,32},{32,48},{48,64},{64,80},{80,96},{96,112},{112,128},... | collective-permute-start | bytes 147464 | tf_op jit(solution)/shard_map/ppermute | solution.py:20
  19.8 1.3 collective-permute-start.1
  21.1 4.2 collective-permute-done.1
  26.3 1.0 fusion.45
  27.6 1.3 collective-permute-start.2
  28.9 4.6 %collective-permute-start.3 = (f32[1,1,6144]{2,1,0:T(1,128)S(1)}, f32[1,1,6144]{2,1,0:T(1,128)S(1)}, u32[]{:S(2)}, u32[]{:S(2)}) collective-permute-start(f32[1,1,6144]{2,1,0:T(1,128)S(1)} %get-tuple-element.99), channel_id=1, source_target_pairs={{0,16},{16,32},{32,48},{48,64},{64,80},{80,96},{96,112},{112,128},... | collective-permute-start | bytes 73736 | tf_op jit(solution)/shard_map/ppermute | solution.py:20
  33.6 0.9 collective-permute-done.3
  34.4 0.9 fusion.36
  35.6 1.3 collective-permute-start.4
  36.9 6.0 %collective-permute-start.5 = (f32[1,1,6144]{2,1,0:T(1,128)S(1)}, f32[1,1,6144]{2,1,0:T(1,128)S(1)}, u32[]{:S(2)}, u32[]{:S(2)}) collective-permute-start(f32[1,1,6144]{2,1,0:T(1,128)S(1)} %get-tuple-element.89), channel_id=1, source_target_pairs={{0,16},{16,32},{32,48},{48,64},{64,80},{80,96},{96,112},{112,128},... | collective-permute-start | bytes 73736 | tf_op jit(solution)/shard_map/ppermute | solution.py:20
  43.0 0.7 collective-permute-done.5
  43.7 0.9 fusion.51
  45.2 12.8 %copy.13 = bf16[1,12,16384]{1,0,2:T(2,128)(2,1)} copy(bf16[1,12,16384]{2,1,0:T(8,128)(2,1)S(1)} %convert_element_type.50) | data formatting | bytes 786432 | tf_op jit(solution)/shard_map/convert_element_type | solution.py:93
  58.5 90.8 %reduce = bf16[16384,12]{1,0:T(8,128)(2,1)} reduce(bf16[16384,1,12]{2,1,0:T(2,128)(2,1)} %bitcast.109, bf16[]{:T(256)} %broadcast.69), dimensions={1}, to_apply=%bitcast.85.reduce_sub_computation | reduce | bytes 786434
  149.3 9.5 %reshape.89 = bf16[16,2,6144]{2,1,0:T(2,128)(2,1)} reshape(bf16[16384,12]{1,0:T(8,128)(2,1)} %reduce) | data formatting | bytes 786432
  158.9 13.1 %all-to-all-start = ((bf16[16,2,6144]{2,1,0:T(2,128)(2,1)}), bf16[16,2,6144]{2,1,0:T(2,128)(2,1)S(1)}, u32[]{:S(2)}, u32[]{:S(2)}) async-start(bf16[16,2,6144]{2,1,0:T(2,128)(2,1)} %reshape.89), calls=%async_computation | async-start | bytes 786432 | tf_op jit(solution)/shard_map/all_to_all | solution.py:92
  172.0 12.3 %all-to-all-done = bf16[16,2,6144]{2,1,0:T(2,128)(2,1)S(1)} async-done(((bf16[16,2,6144]{2,1,0:T(2,128)(2,1)}), bf16[16,2,6144]{2,1,0:T(2,128)(2,1)S(1)}, u32[]{:S(2)}, u32[]{:S(2)}) %all-to-all-start) | async-done | bytes 393248 | tf_op jit(solution)/shard_map/all_to_all | solution.py:92
  184.3 12.2 %reshape.90 = bf16[16384,1,12]{2,1,0:T(2,128)(2,1)} reshape(bf16[16,2,6144]{2,1,0:T(2,128)(2,1)S(1)} %all-to-all-done) | data formatting | bytes 786432
  196.5 15.4 %copy.14 = bf16[1,12,16384]{2,1,0:T(8,128)(2,1)S(1)} copy(bf16[1,12,16384]{1,0,2:T(2,128)(2,1)} %bitcast.110) | data formatting | bytes 786432 | tf_op jit(solution)/shard_map/all_to_all | solution.py:92
  212.9 19.7 %while.10 = (s32[]{:T(128)}, bf16[12,16,1024]{2,1,0:T(8,128)(2,1)S(1)}, bf16[12,16,1024]{2,1,0:T(8,128)(2,1)S(1)}, bf16[384,16]{0,1:T(8,128)(2,1)S(1)}, f32[384]...) while((s32[]{:T(128)}, ...), condition=%wide.region_1.2_spmd, body=%wide.region_0.1_spmd.sunk | while | flops 331907072 | bytes 1962605 | solution.py:98
  213.5 1.0 fusion.83
  214.5 0.6 fusion.82
  215.1 1.0 fusion.83
  216.1 0.6 fusion.82
  216.8 1.0 fusion.83
  217.8 0.6 fusion.82
  218.4 1.0 fusion.83
  220.1 1.0 fusion.83
  221.1 0.6 fusion.82
  221.7 1.0 fusion.83
  223.4 1.0 fusion.83
  224.4 0.6 fusion.82
  225.0 1.0 fusion.83
  226.6 1.0 fusion.83
  227.6 0.6 fusion.82
  228.3 1.0 fusion.83
  229.9 1.0 fusion.83
  230.9 0.6 fusion.82
  231.6 1.0 fusion.83
  232.6 1.1 copy.22
  233.6 4.5 all-to-all-start.1
  238.5 13.4 %all-to-all-done.1 = bf16[16,12,1024]{2,1,0:T(8,128)(2,1)S(1)} async-done(((bf16[16,12,1024]{2,1,0:T(8,128)(2,1)}), bf16[16,12,1024]{2,1,0:T(8,128)(2,1)S(1)}, u32[]{:S(2)}, u32[]{:S(2)}) %all-to-all-start.1) | async-done | bytes 393248 | tf_op jit(solution)/shard_map/all_to_all | solution.py:99
  253.3 1.1 add_select_fusion.1
  255.0 195.6 %all-reduce.2.cloned.1.call-done = f32[12,16384]{1,0:T(8,128)} async-done(((f32[12,16384]{1,0:T(8,128)}), f32[12,16384]{1,0:T(8,128)}) %all-reduce.2.cloned.1.call-update) | async-done | bytes 786448 | tf_op jit(solution)/shard_map/psum | solution.py:31
  450.6 2.2 add_select_fusion
  452.7 1.1 reshape.86
  (49 shorter events, 9.3 us)
Async XLA Ops:
  6.5 8.3 %copy-start = (f32[1,32,6144]{2,1,0:T(8,128)S(1)}, f32[1,32,6144]{2,1,0:T(8,128)}, u32[]{:S(2)}) copy-start(f32[1,32,6144]{2,1,0:T(8,128)} %param.12) | copy-start | bytes 2359300
  14.9 6.1 %collective-permute-start = (f32[2,1,1,6144]{3,2,1,0:T(1,128)S(1)}, f32[2,1,1,6144]{3,2,1,0:T(1,128)S(1)}, u32[]{:S(2)}, u32[]{:S(2)}) collective-permute-start(f32[2,1,1,6144]{3,2,1,0:T(1,128)S(1)} %get-tuple-element.78), channel_id=1, source_target_pairs={{0,16},{16,32},{32,48},{48,64},{64,80},{80,96},{96,112},{112,128},... | collective-permute-start | bytes 147464 | tf_op jit(solution)/shard_map/ppermute | solution.py:20
  19.8 5.5 %collective-permute-start.1 = (f32[2,1,1,6144]{3,2,1,0:T(1,128)S(1)}, f32[2,1,1,6144]{3,2,1,0:T(1,128)S(1)}, u32[]{:S(2)}, u32[]{:S(2)}) collective-permute-start(f32[2,1,1,6144]{3,2,1,0:T(1,128)S(1)} %get-tuple-element.79), channel_id=1, source_target_pairs={{16,0},{32,16},{48,32},{64,48},{80,64},{96,80},{112,96},{128,112},... | collective-permute-start | bytes 147464 | tf_op jit(solution)/shard_map/ppermute | solution.py:22
  27.6 6.0 %collective-permute-start.2 = (f32[1,1,6144]{2,1,0:T(1,128)S(1)}, f32[1,1,6144]{2,1,0:T(1,128)S(1)}, u32[]{:S(2)}, u32[]{:S(2)}) collective-permute-start(f32[1,1,6144]{2,1,0:T(1,128)S(1)} %get-tuple-element.98), channel_id=1, source_target_pairs={{16,0},{32,16},{48,32},{64,48},{80,64},{96,80},{112,96},{128,112},... | collective-permute-start | bytes 73736 | tf_op jit(solution)/shard_map/ppermute | solution.py:22
  28.9 5.6 %collective-permute-start.3 = (f32[1,1,6144]{2,1,0:T(1,128)S(1)}, f32[1,1,6144]{2,1,0:T(1,128)S(1)}, u32[]{:S(2)}, u32[]{:S(2)}) collective-permute-start(f32[1,1,6144]{2,1,0:T(1,128)S(1)} %get-tuple-element.99), channel_id=1, source_target_pairs={{0,16},{16,32},{32,48},{48,64},{64,80},{80,96},{96,112},{112,128},... | collective-permute-start | bytes 73736 | tf_op jit(solution)/shard_map/ppermute | solution.py:20
  35.6 7.4 %collective-permute-start.4 = (f32[1,1,6144]{2,1,0:T(1,128)S(1)}, f32[1,1,6144]{2,1,0:T(1,128)S(1)}, u32[]{:S(2)}, u32[]{:S(2)}) collective-permute-start(f32[1,1,6144]{2,1,0:T(1,128)S(1)} %get-tuple-element.88), channel_id=1, source_target_pairs={{16,0},{32,16},{48,32},{64,48},{80,64},{96,80},{112,96},{128,112},... | collective-permute-start | bytes 73736 | tf_op jit(solution)/shard_map/ppermute | solution.py:22
  36.9 6.8 %collective-permute-start.5 = (f32[1,1,6144]{2,1,0:T(1,128)S(1)}, f32[1,1,6144]{2,1,0:T(1,128)S(1)}, u32[]{:S(2)}, u32[]{:S(2)}) collective-permute-start(f32[1,1,6144]{2,1,0:T(1,128)S(1)} %get-tuple-element.89), channel_id=1, source_target_pairs={{0,16},{16,32},{32,48},{48,64},{64,80},{80,96},{96,112},{112,128},... | collective-permute-start | bytes 73736 | tf_op jit(solution)/shard_map/ppermute | solution.py:20
  158.9 25.4 %all-to-all-start = ((bf16[16,2,6144]{2,1,0:T(2,128)(2,1)}), bf16[16,2,6144]{2,1,0:T(2,128)(2,1)S(1)}, u32[]{:S(2)}, u32[]{:S(2)}) async-start(bf16[16,2,6144]{2,1,0:T(2,128)(2,1)} %reshape.89), calls=%async_computation | async-start | bytes 786432 | tf_op jit(solution)/shard_map/all_to_all | solution.py:92
  211.9 1.0 copy-start.1
  211.9 1.0 copy-start.2
  211.9 0.9 copy-start.3
  211.9 0.9 copy-start.4
  211.9 0.9 copy-start.5
  212.0 0.9 copy-start.6
  233.6 18.3 %all-to-all-start.1 = ((bf16[16,12,1024]{2,1,0:T(8,128)(2,1)}), bf16[16,12,1024]{2,1,0:T(8,128)(2,1)S(1)}, u32[]{:S(2)}, u32[]{:S(2)}) async-start(bf16[16,12,1024]{2,1,0:T(8,128)(2,1)} %bitcast.92), calls=%async_computation.1 | async-start | bytes 1048576 | tf_op jit(solution)/shard_map/all_to_all | solution.py:99
  238.2 212.4 %all-reduce.2.cloned.1.call-start = ((), (), s32[]{:S(2)}) async-start(), calls=%async_computation.2 | async-start | bytes 2097152 | tf_op jit(solution)/shard_map/psum | solution.py:31
  253.2 1.1 copy-start.7
Sparse Core Ops, SparseCore 0:
  254.5 196.0 all-reduce.1
where the time goes:
time: 462 us; the launch traced here: 461 us
  waiting for transfers between devices  227 us (49%)
  other arithmetic  104 us (23%)
  local copies, waits for them, and re-layouts  59.4 us (13%)
  starting transfers between devices  37 us (8%)
  matrix products  19.6 us (4%)
  between operations  13.7 us (3%)
    psum x1, waiting for transfers between devices, from_root(): return lax.psum(block, axis)  196 us
    unnamed x1, other arithmetic  90.8 us
    unnamed x22, local copies, waits for them, and re-layouts  23.9 us
    ppermute x3, starting transfers between devices, extended(): lax.ppermute(tail, axis, [(i, (i + 1) % count) for i in range(ends)])  15.5 us
    all_to_all x1, local copies, waits for them, and re-layouts, on_device(): lax.all_to_all(by_block.astype(jnp.bfloat16), 'field', split_axis=2, conc...  15.4 us
    all_to_all x1, waiting for transfers between devices, on_device(): lax.all_to_all(change, 'field', split_axis=0, concat_axis=2, tiled=True)  13.4 us
    convert_element_type x2, local copies, waits for them, and re-layouts, on_device(): by_block.astype(jnp.bfloat16)  13.4 us
    all_to_all x1, starting transfers between devices, on_device(): lax.all_to_all(by_block.astype(jnp.bfloat16), 'field', split_axis=2, conc...  13.1 us
  transfers between devices with their start and end apart: 9, of which 6 were waited for; matrix products, arithmetic and copies ran while one was open for 0% of the time, Pallas kernels for 0%

commit v1 on v0

--- a/solution.py
+++ b/solution.py
@@ -28,7 +28,7 @@
 
 def from_root(block, axis, holder):
     block = jnp.where(lax.axis_index(axis) == holder, block, jnp.zeros_like(block))
-    return lax.psum(block, axis)
+    return jnp.sum(lax.all_gather(block, axis), axis=0)
 
 
 def relax_step(padded, source, coef_pad, weight):

time: 462 us -> 489 us (1.058)
  matrix products: 19.6 us -> 43.5 us
  waiting for transfers between devices: 227 us -> 216 us
  other arithmetic: 104 us -> 113 us
    psum x1 -> x0, waiting for transfers between devices: 196 us -> none  [from_root(): return lax.psum(block, axis)]
    all_gather x0 -> x1, waiting for transfers between devices: none -> 184 us  [from_root(): return jnp.sum(lax.all_gather(block, axis), axis=0)]
    dot_general x12, matrix products: 12 us -> 25.4 us  [one_block(): jnp.dot(weight_out, hidden, preferred_element_type=jnp.float32)]
    dot_general x12, matrix products: 7.58 us -> 18.2 us  [one_block(): jnp.dot(weight_in, row_block, preferred_element_type=jnp.float32)]
    reduce_sum x0 -> x1, other arithmetic: none -> 6.86 us  [from_root(): return jnp.sum(lax.all_gather(block, axis), axis=0)]
    convert_element_type x1 -> x4, local copies, waits for them, and re-layouts: 0.46 us -> 5.42 us  [on_device(): lax.all_to_all(change, 'field', split_axis=0, concat_axis=2, tiled=True)]
    unnamed x22 -> x18, local copies, waits for them, and re-layouts: 23.9 us -> 22.9 us
    convert_element_type x2 -> x1, local copies, waits for them, and re-layouts: 13.4 us -> 12.9 us  [on_device(): by_block.astype(jnp.bfloat16)]
  transfers between devices with their start and end apart: 9 -> 9, of which waited for: 6 -> 6; matrix products, arithmetic and copies ran while one was open for 0% -> 1% of each run, Pallas kernels for 0% -> 0%
where the time goes in v1:
time: 489 us; the launch traced here: 485 us
  waiting for transfers between devices  216 us (44%)
  other arithmetic  113 us (23%)
  local copies, waits for them, and re-layouts  62.1 us (13%)
  matrix products  43.5 us (9%)
  starting transfers between devices  37.2 us (8%)
  between operations  13.6 us (3%)
    all_gather x1, waiting for transfers between devices, from_root(): return jnp.sum(lax.all_gather(block, axis), axis=0)  184 us
    unnamed x1, other arithmetic  90.8 us
    dot_general x12, matrix products, one_block(): jnp.dot(weight_out, hidden, preferred_element_type=jnp.float32)  25.4 us
    unnamed x18, local copies, waits for them, and re-layouts  22.9 us
    dot_general x12, matrix products, one_block(): jnp.dot(weight_in, row_block, preferred_element_type=jnp.float32)  18.2 us
    ppermute x3, starting transfers between devices, extended(): lax.ppermute(tail, axis, [(i, (i + 1) % count) for i in range(ends)])  15.5 us
    all_to_all x1, local copies, waits for them, and re-layouts, on_device(): lax.all_to_all(by_block.astype(jnp.bfloat16), 'field', split_axis=2, conc...  15.4 us
    all_to_all x1, waiting for transfers between devices, on_device(): lax.all_to_all(change, 'field', split_axis=0, concat_axis=2, tiled=True)  13.7 us
  transfers between devices with their start and end apart: 9, of which 6 were waited for; matrix products, arithmetic and copies ran while one was open for 1% of the time, Pallas kernels for 0%

profile of v1, /device:TPU:1, one launch (start us, length us, event | category | flops | bytes accessed | tf_op | source)
XLA Modules:
  0.0 485.4 jit_solution(2256536463914739264)
XLA Ops:
  6.5 1.6 fusion.63
  8.2 6.8 %add_bitcast_fusion = f32[1,1,32,6144]{3,2,1,0:T(8,128)S(1)} fusion(s32[32,6144]{1,0:T(8,128)} %param.13, f32[]{:T(128)} %bitcast.13, f32[]{:T(128)} %bitcast.12, f32[]{:T(128)} %bitcast.11, f32[]{:T(128)} %bitcast.10, f32[]{:T(128)} %bitcast.9, f32[]{:T(128)} %bitcast.8, f32[]{:T(128)} %bitcast.7, f32[]{:T(128)} %bitcast.6), kind=kLoop, calls=%fused_computation.79 | loop fusion | flops 4521984 | bytes 1572896 | tf_op jit(solution)/shard_map/stack | solution.py:70
  15.1 4.8 collective-permute-start
  19.9 1.3 collective-permute-start.1
  21.2 4.2 collective-permute-done.1
  27.7 1.3 collective-permute-start.2
  29.0 4.6 collective-permute-start.3
  37.1 6.0 %collective-permute-start.5 = (f32[1,1,6144]{2,1,0:T(1,128)S(1)}, f32[1,1,6144]{2,1,0:T(1,128)S(1)}, u32[]{:S(2)}, u32[]{:S(2)}) collective-permute-start(f32[1,1,6144]{2,1,0:T(1,128)S(1)} %get-tuple-element.91), channel_id=1, source_target_pairs={{0,16},{16,32},{32,48},{48,64},{64,80},{80,96},{96,112},{112,128},... | collective-permute-start | bytes 73736 | tf_op jit(solution)/shard_map/ppermute | solution.py:20
  45.1 12.9 %copy.17 = bf16[1,12,16384]{1,0,2:T(2,128)(2,1)} copy(bf16[1,12,16384]{2,1,0:T(8,128)(2,1)S(1)} %convert_element_type.84) | data formatting | bytes 786432 | tf_op jit(solution)/shard_map/convert_element_type | solution.py:93
  58.5 90.8 %reduce = bf16[16384,12]{1,0:T(8,128)(2,1)} reduce(bf16[16384,1,12]{2,1,0:T(2,128)(2,1)} %bitcast.109, bf16[]{:T(256)} %broadcast.91), dimensions={1}, to_apply=%bitcast.86.reduce_sub_computation | reduce | bytes 786434
  149.3 9.5 %reshape.152 = bf16[16,2,6144]{2,1,0:T(2,128)(2,1)} reshape(bf16[16384,12]{1,0:T(8,128)(2,1)} %reduce) | data formatting | bytes 786432
  158.8 13.1 %all-to-all-start = ((bf16[16,2,6144]{2,1,0:T(2,128)(2,1)}), bf16[16,2,6144]{2,1,0:T(2,128)(2,1)S(1)}, u32[]{:S(2)}, u32[]{:S(2)}) async-start(bf16[16,2,6144]{2,1,0:T(2,128)(2,1)} %reshape.152), calls=%async_computation | async-start | bytes 786432 | tf_op jit(solution)/shard_map/all_to_all | solution.py:92
  171.9 12.3 %all-to-all-done = bf16[16,2,6144]{2,1,0:T(2,128)(2,1)S(1)} async-done(((bf16[16,2,6144]{2,1,0:T(2,128)(2,1)}), bf16[16,2,6144]{2,1,0:T(2,128)(2,1)S(1)}, u32[]{:S(2)}, u32[]{:S(2)}) %all-to-all-start) | async-done | bytes 393248 | tf_op jit(solution)/shard_map/all_to_all | solution.py:92
  184.2 12.2 %reshape.153 = bf16[16384,1,12]{2,1,0:T(2,128)(2,1)} reshape(bf16[16,2,6144]{2,1,0:T(2,128)(2,1)S(1)} %all-to-all-done) | data formatting | bytes 786432
  196.4 15.4 %copy.18 = bf16[1,12,16384]{2,1,0:T(8,128)(2,1)S(1)} copy(bf16[1,12,16384]{1,0,2:T(2,128)(2,1)} %bitcast.110) | data formatting | bytes 786432 | tf_op jit(solution)/shard_map/all_to_all | solution.py:92
  212.6 43.6 %while.10 = (s32[]{:T(128)}, bf16[12,16,1024]{2,1,0:T(8,128)(2,1)S(1)}, bf16[12,16,1024]{2,1,0:T(8,128)(2,1)S(1)}, bf16[384,16]{0,1:T(8,128)(2,1)S(1)}, f32[384]...) while((s32[]{:T(128)}, ...), condition=%wide.region_1.2_spmd, body=%wide.region_0.1_spmd.sunk | while | flops 331907072 | bytes 3142289 | solution.py:98
  212.6 1.5 fusion.80
  214.1 2.1 fusion.81
  216.2 1.5 fusion.80
  217.7 2.1 fusion.81
  219.8 1.5 fusion.80
  221.4 2.1 fusion.81
  223.5 1.5 fusion.80
  225.0 2.1 fusion.81
  227.1 1.5 fusion.80
  228.6 2.1 fusion.81
  230.8 1.5 fusion.80
  232.3 2.1 fusion.81
  234.4 1.5 fusion.80
  235.9 2.1 fusion.81
  238.0 1.5 fusion.80
  239.6 2.1 fusion.81
  241.7 1.5 fusion.80
  243.2 2.1 fusion.81
  245.3 1.5 fusion.80
  246.8 2.1 fusion.81
  248.9 1.5 fusion.80
  250.5 2.1 fusion.81
  252.6 1.5 fusion.80
  254.1 2.1 fusion.81
  257.3 4.8 all-to-all-start.1
  262.1 13.7 %all-to-all-done.1 = bf16[16,12,1024]{2,1,0:T(8,128)(2,1)S(1)} async-done(((bf16[16,12,1024]{2,1,0:T(8,128)(2,1)}), bf16[16,12,1024]{2,1,0:T(8,128)(2,1)S(1)}, u32[]{:S(2)}, u32[]{:S(2)}) %all-to-all-start.1) | async-done | bytes 393248 | tf_op jit(solution)/shard_map/all_to_all | solution.py:99
  275.9 1.3 copy.20
  277.3 2.4 reshape.151
  279.7 2.3 add_select_fusion
  284.5 184.1 %all-gather.2.cloned.1.call-done = f32[16,12,16384]{2,1,0:T(8,128)} async-done(((f32[1,12,16384]{2,1,0:T(8,128)}), f32[16,12,16384]{2,1,0:T(8,128)}) %all-gather.2.cloned.1.call-update) | async-done | bytes 12582928 | tf_op jit(solution)/shard_map/all_gather | solution.py:31
  468.6 6.9 %reduce_sum.11 = f32[12,16384]{1,0:T(8,128)S(1)} reduce(f32[16,12,16384]{2,1,0:T(8,128)} %all-gather.2.cloned.1.call-done, f32[]{:T(128)} %constant.8.clone.1), dimensions={0}, to_apply=%region_2.3 | reduce | flops 2949120 | bytes 13369348 | tf_op jit(solution)/shard_map/reduce_sum | solution.py:31
  475.7 2.9 add_select_fusion.1
  (73 shorter events, 12.9 us)
Async XLA Ops:
  6.5 8.4 %copy-start = (f32[1,32,6144]{2,1,0:T(8,128)S(1)}, f32[1,32,6144]{2,1,0:T(8,128)}, u32[]{:S(2)}) copy-start(f32[1,32,6144]{2,1,0:T(8,128)} %param.12) | copy-start | bytes 2359300
  15.1 6.1 %collective-permute-start = (f32[2,1,1,6144]{3,2,1,0:T(1,128)S(1)}, f32[2,1,1,6144]{3,2,1,0:T(1,128)S(1)}, u32[]{:S(2)}, u32[]{:S(2)}) collective-permute-start(f32[2,1,1,6144]{3,2,1,0:T(1,128)S(1)} %get-tuple-element.76), channel_id=1, source_target_pairs={{0,16},{16,32},{32,48},{48,64},{64,80},{80,96},{96,112},{112,128},... | collective-permute-start | bytes 147464 | tf_op jit(solution)/shard_map/ppermute | solution.py:20
  19.9 5.5 %collective-permute-start.1 = (f32[2,1,1,6144]{3,2,1,0:T(1,128)S(1)}, f32[2,1,1,6144]{3,2,1,0:T(1,128)S(1)}, u32[]{:S(2)}, u32[]{:S(2)}) collective-permute-start(f32[2,1,1,6144]{3,2,1,0:T(1,128)S(1)} %get-tuple-element.77), channel_id=1, source_target_pairs={{16,0},{32,16},{48,32},{64,48},{80,64},{96,80},{112,96},{128,112},... | collective-permute-start | bytes 147464 | tf_op jit(solution)/shard_map/ppermute | solution.py:22
  27.7 6.0 %collective-permute-start.2 = (f32[1,1,6144]{2,1,0:T(1,128)S(1)}, f32[1,1,6144]{2,1,0:T(1,128)S(1)}, u32[]{:S(2)}, u32[]{:S(2)}) collective-permute-start(f32[1,1,6144]{2,1,0:T(1,128)S(1)} %get-tuple-element.96), channel_id=1, source_target_pairs={{16,0},{32,16},{48,32},{64,48},{80,64},{96,80},{112,96},{128,112},... | collective-permute-start | bytes 73736 | tf_op jit(solution)/shard_map/ppermute | solution.py:22
  29.0 5.6 %collective-permute-start.3 = (f32[1,1,6144]{2,1,0:T(1,128)S(1)}, f32[1,1,6144]{2,1,0:T(1,128)S(1)}, u32[]{:S(2)}, u32[]{:S(2)}) collective-permute-start(f32[1,1,6144]{2,1,0:T(1,128)S(1)} %get-tuple-element.97), channel_id=1, source_target_pairs={{0,16},{16,32},{32,48},{48,64},{64,80},{80,96},{96,112},{112,128},... | collective-permute-start | bytes 73736 | tf_op jit(solution)/shard_map/ppermute | solution.py:20
  35.8 7.4 %collective-permute-start.4 = (f32[1,1,6144]{2,1,0:T(1,128)S(1)}, f32[1,1,6144]{2,1,0:T(1,128)S(1)}, u32[]{:S(2)}, u32[]{:S(2)}) collective-permute-start(f32[1,1,6144]{2,1,0:T(1,128)S(1)} %get-tuple-element.90), channel_id=1, source_target_pairs={{16,0},{32,16},{48,32},{64,48},{80,64},{96,80},{112,96},{128,112},... | collective-permute-start | bytes 73736 | tf_op jit(solution)/shard_map/ppermute | solution.py:22
  37.1 6.8 %collective-permute-start.5 = (f32[1,1,6144]{2,1,0:T(1,128)S(1)}, f32[1,1,6144]{2,1,0:T(1,128)S(1)}, u32[]{:S(2)}, u32[]{:S(2)}) collective-permute-start(f32[1,1,6144]{2,1,0:T(1,128)S(1)} %get-tuple-element.91), channel_id=1, source_target_pairs={{0,16},{16,32},{32,48},{48,64},{64,80},{80,96},{96,112},{112,128},... | collective-permute-start | bytes 73736 | tf_op jit(solution)/shard_map/ppermute | solution.py:20
  158.8 25.4 %all-to-all-start = ((bf16[16,2,6144]{2,1,0:T(2,128)(2,1)}), bf16[16,2,6144]{2,1,0:T(2,128)(2,1)S(1)}, u32[]{:S(2)}, u32[]{:S(2)}) async-start(bf16[16,2,6144]{2,1,0:T(2,128)(2,1)} %reshape.152), calls=%async_computation | async-start | bytes 786432 | tf_op jit(solution)/shard_map/all_to_all | solution.py:92
  211.9 0.7 copy-start.2
  211.9 0.7 copy-start.3
  211.9 0.7 copy-start.4
  211.9 0.7 copy-start.5
  211.9 0.7 copy-start.6
  212.6 1.5 copy-start.1
  216.2 1.5 copy-start.1
  219.8 1.5 copy-start.1
  223.5 1.5 copy-start.1
  227.1 1.5 copy-start.1
  230.8 1.5 copy-start.1
  234.4 1.5 copy-start.1
  238.0 1.5 copy-start.1
  241.7 1.5 copy-start.1
  245.3 1.5 copy-start.1
  248.9 1.5 copy-start.1
  252.6 1.5 copy-start.1
  257.3 18.5 %all-to-all-start.1 = ((bf16[16,12,1024]{2,1,0:T(8,128)(2,1)}), bf16[16,12,1024]{2,1,0:T(8,128)(2,1)S(1)}, u32[]{:S(2)}, u32[]{:S(2)}) async-start(bf16[16,12,1024]{2,1,0:T(8,128)(2,1)} %bitcast.92), calls=%async_computation.1 | async-start | bytes 1048576 | tf_op jit(solution)/shard_map/all_to_all | solution.py:99
  262.0 206.6 %all-gather.2.cloned.1.call-start = ((), (), s32[]{:S(2)}) async-start(), calls=%async_computation.2 | async-start | bytes 17825792 | tf_op jit(solution)/shard_map/all_gather | solution.py:31
  279.7 2.4 copy-start.7
Sparse Core Ops, SparseCore 0:
  282.2 186.4 all-gather.1
